TPU v7x, 32 devices: a whole 2x2x4 slice. The times are simulated.
32 devices in a mesh: dp: 8 (over y, x, core), blk: 4 (over z).
Axes of the slice: x: 2, y: 2, z: 4, core: 2. Of those that a mesh axis runs over, the one named last changes fastest.
Arguments:
- spans: bfloat16 [40960, 1024], P(('dp', 'blk')), may hold values from -6 to 6
- span_counts: int32 [32], P(('dp', 'blk')), may hold values from 16 to 1232, as said below
- session_ids: int32 [40960], P(('dp', 'blk')), may hold values from 0 to 15, as said below
- destinations: int32 [40960], P(('dp', 'blk')), may hold values from 0 to 7, as said below
- expert_weight: bfloat16 [8, 1024, 4096], P('dp'), may hold values from -0.1875 to 0.1875
- norm_gain: float32 [1024], replicated, may hold values from 0.1 to 1.9
- queries: bfloat16 [28672, 4096], P(('dp', 'blk')), may hold values from -6 to 6
- positives: int32 [28672], P(('dp', 'blk')), may hold values from 0 to 63
Outputs:
- loss_rows: float32 [28672], P(('dp', 'blk'))
- grad_queries: bfloat16 [28672, 4096], P(('dp', 'blk'))
- grad_sessions: float32 [512, 4096], P(('dp', 'blk'))
Inputs may be any that keep to these rules, and one draw needn't show every extreme that they name: `span_counts`: for each blk index the counts of the devices along dp sum to 2560, and one of them has the largest value. `destinations`: the live rows of the devices that share a blk index, in order of dp index and then of row, name the experts in cyclic order from a drawn start: each expert receives exactly 320 live rows of its blk index, and a device sends at most 154 live rows to one expert, the device with the largest count exactly 154 to each. Rows at or after a device's count name any expert. `session_ids`: on each device the ids of the live rows never fall, begin at 0 and take every value; rows at or after the count carry any id.
All inputs are finite; a program needn't handle non-finite values.
Results may differ from a plain program's by a relative error of at most 0.0072.
Values may be sent and summed in bfloat16 or wider, within the bound.
No kernel may reach another device: no remote copies, remote signals or barrier semaphores. Data moves between devices by JAX's collectives and lax.ppermute only.
A program may use at most 128 MiB of HBM per device.

v0:
```python
import jax
import jax.numpy as jnp
from jax import lax
from jax.sharding import PartitionSpec as P

SESS_DEV = 16
logit_scale = 20.0
epsilon = 1e-06


def passed_along(shard, axis, by):
    length = lax.axis_size(axis)
    return lax.ppermute(shard, axis, [(i, (i + by) % length) for i in range(length)])


def unit_rows(values):
    widened = values.astype(jnp.float32)
    return (
        widened * lax.rsqrt(jnp.sum(widened * widened, axis=-1, keepdims=True) + epsilon)
    ).astype(jnp.bfloat16)


def contract_rows(left_side, right_side):
    return lax.dot_general(
        left_side, right_side, (((1,), (1,)), ((), ())), preferred_element_type=jnp.float32
    )


def contract_first(left_side, right_side):
    return lax.dot_general(
        left_side, right_side, (((0,), (0,)), ((), ())), preferred_element_type=jnp.float32
    )


def on_device(
    spans, span_counts, session_ids, destinations, expert_weight, norm_gain, queries, positives
):
    rows_dev = spans.shape[0]
    hidden_width = spans.shape[1]
    groups = lax.axis_size("dp")
    capacity = (rows_dev - 3 * SESS_DEV) // groups
    received = rows_dev // 4
    live_rows = jnp.arange(rows_dev, dtype=jnp.int32) < span_counts[0]
    expert_ids = jnp.arange(groups, dtype=jnp.int32)
    expert_marks = ((destinations[:, None] == expert_ids[None, :]) & live_rows[:, None]).astype(
        jnp.int32
    )
    before = jnp.cumsum(expert_marks, axis=0) - expert_marks
    slot_index = jnp.where(
        live_rows,
        destinations * capacity + jnp.sum(before * expert_marks, axis=1),
        groups * capacity,
    )
    send_counts = jnp.sum(expert_marks, axis=0)
    send_rows = (
        jnp.zeros((groups * capacity, hidden_width), jnp.bfloat16)
        .at[slot_index]
        .set(spans, mode="drop")
        .reshape(groups, capacity, hidden_width)
    )
    slot_session = (
        jnp.full((groups * capacity,), -1, jnp.int32).at[slot_index].set(session_ids, mode="drop")
    )
    got_rows, got_counts = (
        lax.all_to_all(send_rows, "dp", split_axis=0, concat_axis=0, tiled=True),
        lax.all_to_all(send_counts, "dp", split_axis=0, concat_axis=0, tiled=True),
    )
    slot_rank = jnp.arange(capacity, dtype=jnp.int32)
    valid_slots = slot_rank[None, :] < got_counts[:, None]
    packed_at = jnp.where(
        valid_slots, (jnp.cumsum(got_counts) - got_counts)[:, None] + slot_rank[None, :], received
    ).reshape(groups * capacity)
    packed = (
        jnp.zeros((received, hidden_width), jnp.bfloat16)
        .at[packed_at]
        .set(got_rows.reshape(groups * capacity, hidden_width), mode="drop")
    )
    widened = packed.astype(jnp.float32)
    normed = (
        widened
        * lax.rsqrt(jnp.mean(widened * widened, axis=-1, keepdims=True) + epsilon)
        * norm_gain
    ).astype(jnp.bfloat16)
    embedded = jax.nn.gelu(
        jnp.dot(normed, expert_weight[0], preferred_element_type=jnp.float32), approximate=True
    ).astype(jnp.bfloat16)
    emb_width = embedded.shape[1]
    gather_at = jnp.minimum(packed_at, received - 1)
    outgoing = jnp.where(
        valid_slots.reshape(groups * capacity)[:, None],
        embedded[gather_at],
        jnp.zeros((), jnp.bfloat16),
    ).reshape(groups, capacity, emb_width)
    returned = lax.all_to_all(outgoing, "dp", split_axis=0, concat_axis=0, tiled=True)
    selector = (jnp.arange(SESS_DEV, dtype=jnp.int32)[:, None] == slot_session[None, :]).astype(
        jnp.bfloat16
    )
    pooled = jnp.dot(
        selector, returned.reshape(groups * capacity, emb_width), preferred_element_type=jnp.float32
    )
    doc_unit = unit_rows(pooled)
    query_unit = unit_rows(queries)
    doc_rows = doc_unit.shape[0]
    doc_piece = lax.all_gather(doc_unit, "blk", axis=0, tiled=True)
    piece_rows = doc_piece.shape[0]
    logits = logit_scale * contract_rows(query_unit, doc_piece)
    weights = jnp.exp(logits)
    inside = (positives >= 0) & (positives < piece_rows)
    matches = positives[:, None] == jnp.arange(piece_rows, dtype=jnp.int32)[None, :]
    picked = doc_piece[jnp.clip(positives, 0, piece_rows - 1)].astype(jnp.float32)
    totals = jnp.sum(weights, axis=1)
    numerator = jnp.dot(weights.astype(jnp.bfloat16), doc_piece, preferred_element_type=jnp.float32)
    chosen_logit = jnp.sum(jnp.where(matches, logits, 0.0), axis=1)
    chosen_doc = jnp.where(inside[:, None], picked, 0.0)
    cycle_size = lax.axis_size("blk")
    position = lax.axis_index("blk")

    def backward(step_index, running):
        travelling, accumulated = running
        row_start = (position - step_index) % cycle_size * doc_rows
        logits = logit_scale * contract_rows(query_unit, travelling)
        matches = (positives - row_start)[:, None] == jnp.arange(doc_rows, dtype=jnp.int32)[None, :]
        coefficient = (jnp.exp(logits) / totals[:, None] - matches.astype(jnp.float32)).astype(
            jnp.bfloat16
        )
        accumulated = accumulated + logit_scale * contract_first(coefficient, query_unit)
        travelling = passed_along(travelling, "blk", 1)
        accumulated = passed_along(accumulated, "blk", 1)
        return (travelling, accumulated)

    grad_docs = lax.fori_loop(
        0, cycle_size, backward, (doc_unit, jnp.zeros((doc_rows, emb_width), jnp.float32))
    )[1]
    loss_rows = jnp.log(totals) - chosen_logit
    grad_queries = (logit_scale * (numerator / totals[:, None] - chosen_doc)).astype(jnp.bfloat16)
    return (loss_rows, grad_queries, grad_docs)


def solution(mesh):
    placed = (
        P(("dp", "blk"), None),
        P(("dp", "blk")),
        P(("dp", "blk")),
        P(("dp", "blk")),
        P("dp", None, None),
        P(),
        P(("dp", "blk"), None),
        P(("dp", "blk")),
    )
    return jax.shard_map(
        on_device,
        mesh=mesh,
        in_specs=placed,
        out_specs=(P(("dp", "blk")), P(("dp", "blk"), None), P(("dp", "blk"), None)),
        check_vma=False,
    )
```

profile of v0, /device:TPU:0, one launch (start us, length us, event | category | flops | bytes accessed | tf_op | source)
XLA Modules:
  0.0 356.3 jit_solution(18068380321817378988)
XLA Ops:
  12.2 9.7 %scatter_custom_fusion.1 = bf16[1232,1024]{1,0:T(8,128)(2,1)S(1)} fusion(s32[1280]{0:T(1024)S(1)} %compare_select_fusion.2, bf16[1280,1024]{1,0:T(8,128)(2,1)} %param.10, bf16[]{:T(256)} %constant.108.clone.1), kind=kCustom, calls=%fused_computation.41 | custom fusion | bytes 2523648 | tf_op jit(solution)/shard_map/scatter | solution.py:58
  28.7 31.5 %all-to-all-done.1 = bf16[8,154,1024]{2,1,0:T(8,128)(2,1)S(1)} async-done(((bf16[8,154,1024]{2,1,0:T(8,128)(2,1)}), bf16[8,154,1024]{2,1,0:T(8,128)(2,1)S(1)}, u32[]{:S(2)}, u32[]{:S(2)}) %all-to-all-start.1) | async-done | bytes 2523168 | tf_op jit(solution)/shard_map/all_to_all | solution.py:65
  62.0 9.5 %scatter_custom_fusion.2 = bf16[320,1024]{1,0:T(8,128)(2,1)S(1)} fusion(s32[1232]{0:T(1024)S(1)} %get-tuple-element.186, bf16[1232,1024]{1,0:T(8,128)(2,1)} %reshape.246, bf16[]{:T(256)} %constant.108.clone.1), kind=kCustom, calls=%fused_computation.46 | custom fusion | bytes 655872 | tf_op jit(solution)/shard_map/scatter | solution.py:76
  71.8 7.3 %fusion.21 = bf16[320,4096]{1,0:T(8,128)(2,1)S(1)} fusion(bf16[1,1024,4096]{2,1,0:T(8,128)(2,1)} %param.14, bf16[320,1024]{1,0:T(8,128)(2,1)S(1)} %scatter_custom_fusion.2, f32[1024]{0:T(1024)S(1)} %copy-done.2, f32[320]{0:T(512)S(1)} %add_rsqrt_fusion.1), kind=kOutput, calls=%fused_computation.35 | convolution fusion | flops 2697461760 | bytes 11670784 | tf_op jit(solution)/shard_map/dot_general | solution.py:85
  79.1 8.2 %gather_fusion = bf16[1232,4096]{1,0:T(8,128)(2,1)} fusion(bf16[320,4096]{1,0:T(8,128)(2,1)S(1)} %fusion.21, s32[2048]{0:T(1024)S(1)} %pad_clamp_fusion), kind=kCustom, calls=%fused_computation | custom fusion | bytes 20190016 | tf_op jit(solution)/shard_map/gather | solution.py:91
  87.4 12.1 %gather.9 = bf16[8,154,4096]{2,1,0:T(8,128)(2,1)} reshape(bf16[1232,4096]{1,0:T(8,128)(2,1)} %gather_fusion) | data formatting | bytes 20185088 | tf_op jit(solution)/shard_map/gather | solution.py:91
  99.5 10.0 %broadcast_select_fusion = bf16[8,154,4096]{2,1,0:T(8,128)(2,1)} fusion(bf16[8,154,4096]{2,1,0:T(8,128)(2,1)} %gather.9, pred[8,154]{1,0:T(8,128)(4,1)S(1)} %iota_compare_fusion.7), kind=kLoop, calls=%fused_computation.24 | loop fusion | flops 5046272 | bytes 20186320 | tf_op jit(solution)/shard_map/jit(_where)/select_n | solution.py:89
  114.8 5.6 %scatter_custom_fusion = s32[1232]{0:T(1024)S(1)} fusion(s32[1280]{0:T(1024)S(1)} %compare_select_fusion.2, s32[1280]{0:T(1024)} %param.12, s32[]{:T(128)} %constant.103.clone.1), kind=kCustom, calls=%fused_computation.82 | custom fusion | bytes 5440 | tf_op jit(solution)/shard_map/scatter | solution.py:62
  125.0 9.0 %fusion.11 = bf16[896,4096]{1,0:T(8,128)(2,1)} fusion(bf16[896,4096]{1,0:T(8,128)(2,1)} %param.16, f32[896]{0:T(1024)S(1)} %add_rsqrt_fusion), kind=kLoop, calls=%fused_computation.22 | loop fusion | flops 11010048 | bytes 14683648 | tf_op jit(solution)/shard_map/convert_element_type | solution.py:20
  134.0 97.3 %all-to-all-done.2 = bf16[8,154,4096]{2,1,0:T(8,128)(2,1)} async-done(((bf16[8,154,4096]{2,1,0:T(8,128)(2,1)}), bf16[8,154,4096]{2,1,0:T(8,128)(2,1)}, u32[]{:S(2)}, u32[]{:S(2)}) %all-to-all-start.2) | async-done | bytes 10092576 | tf_op jit(solution)/shard_map/all_to_all | solution.py:94
  231.3 12.2 %reshape.209 = bf16[1232,4096]{1,0:T(8,128)(2,1)} reshape(bf16[8,154,4096]{2,1,0:T(8,128)(2,1)} %all-to-all-done.2) | data formatting | bytes 20185088 | tf_op jit(solution)/shard_map/reshape | solution.py:99
  243.4 5.5 %multiply_reduce_fusion = (f32[16]{0:T(128)S(1)}, f32[16,4096]{1,0:T(8,128)S(1)}) fusion(bf16[1232,4096]{1,0:T(8,128)(2,1)} %reshape.209, s32[1232]{0:T(1024)S(1)} %scatter_custom_fusion), kind=kOutput, calls=%fused_computation.49 | convolution fusion | flops 161631472 | bytes 10359680 | tf_op jit(solution)/shard_map/dot_general | solution.py:98
  249.1 16.4 %all_gather.3 = bf16[64,4096]{1,0:T(8,128)(2,1)S(1)} all-gather(bf16[16,4096]{1,0:T(8,128)(2,1)S(1)} %multiply_convert_fusion.1), channel_id=1, replica_groups=mesh['dp'=8,'blk'=4] {'blk'}, dimensions={0}, use_global_device_ids=true | all-gather | bytes 655360 | tf_op jit(solution)/shard_map/all_gather | solution.py:104
  267.9 73.3 %while.17 = (s32[]{:T(128)}, bf16[16,4096]{1,0:T(8,128)(2,1)S(1)}, f32[16,4096]{1,0:T(8,128)S(1)}, bf16[896,4096]{1,0:T(8,128)(2,1)}, f32[896]{0:T(1024)S(1)}, /...) while((s32[]{:T(128)}, bf16[16,4096]{1,0:T(8,128)(2,1)S(1)}, ...), condition=%wide.region_14.15_spmd, body=%wide.region_13.14_spmd.sunk | while | flops 235099024 | bytes 9845070 | solution.py:131
  268.0 8.7 %fusion.59 = f32[16,4096]{1,0:T(8,128)S(1)} fusion(f32[16,4096]{1,0:T(8,128)S(1)} %get-tuple-element.261, bf16[896,4096]{1,0:T(8,128)(2,1)} %get-tuple-element.274, bf16[16,4096]{1,0:T(8,128)(2,1)S(1)} %copy.20, s32[896]{0:T(1024)S(1)} %broadcast_subtract_fusion.2, f32[896]{0:T(1024)S(1)} %get-tuple-element.275), kind=kOutput, calls=%fused_computation.6.clone.1 | convolution fusion | flops 235098112 | bytes 8002560 | tf_op jit(solution)/shard_map/while/body/eval_jaxpr/dot_general | solution.py:30
  278.0 8.3 %collective-permute-done = bf16[16,4096]{1,0:T(8,128)(2,1)S(1)} collective-permute-done((bf16[16,4096]{1,0:T(8,128)(2,1)S(1)}, bf16[16,4096]{1,0:T(8,128)(2,1)S(1)}, u32[]{:S(2)}, u32[]{:S(2)}) %collective-permute-start) | collective-permute-done | bytes 131104 | tf_op jit(solution)/shard_map/while/body/eval_jaxpr/ppermute | solution.py:13
  286.3 8.7 %fusion.59 = f32[16,4096]{1,0:T(8,128)S(1)} fusion(f32[16,4096]{1,0:T(8,128)S(1)} %get-tuple-element.261, bf16[896,4096]{1,0:T(8,128)(2,1)} %get-tuple-element.274, bf16[16,4096]{1,0:T(8,128)(2,1)S(1)} %copy.20, s32[896]{0:T(1024)S(1)} %broadcast_subtract_fusion.2, f32[896]{0:T(1024)S(1)} %get-tuple-element.275), kind=kOutput, calls=%fused_computation.6.clone.1 | convolution fusion | flops 235098112 | bytes 8002560 | tf_op jit(solution)/shard_map/while/body/eval_jaxpr/dot_general | solution.py:30
  295.1 9.5 %collective-permute-done = bf16[16,4096]{1,0:T(8,128)(2,1)S(1)} collective-permute-done((bf16[16,4096]{1,0:T(8,128)(2,1)S(1)}, bf16[16,4096]{1,0:T(8,128)(2,1)S(1)}, u32[]{:S(2)}, u32[]{:S(2)}) %collective-permute-start) | collective-permute-done | bytes 131104 | tf_op jit(solution)/shard_map/while/body/eval_jaxpr/ppermute | solution.py:13
  304.6 8.7 %fusion.59 = f32[16,4096]{1,0:T(8,128)S(1)} fusion(f32[16,4096]{1,0:T(8,128)S(1)} %get-tuple-element.261, bf16[896,4096]{1,0:T(8,128)(2,1)} %get-tuple-element.274, bf16[16,4096]{1,0:T(8,128)(2,1)S(1)} %copy.20, s32[896]{0:T(1024)S(1)} %broadcast_subtract_fusion.2, f32[896]{0:T(1024)S(1)} %get-tuple-element.275), kind=kOutput, calls=%fused_computation.6.clone.1 | convolution fusion | flops 235098112 | bytes 8002560 | tf_op jit(solution)/shard_map/while/body/eval_jaxpr/dot_general | solution.py:30
  313.4 9.5 %collective-permute-done = bf16[16,4096]{1,0:T(8,128)(2,1)S(1)} collective-permute-done((bf16[16,4096]{1,0:T(8,128)(2,1)S(1)}, bf16[16,4096]{1,0:T(8,128)(2,1)S(1)}, u32[]{:S(2)}, u32[]{:S(2)}) %collective-permute-start) | collective-permute-done | bytes 131104 | tf_op jit(solution)/shard_map/while/body/eval_jaxpr/ppermute | solution.py:13
  323.0 8.7 %fusion.59 = f32[16,4096]{1,0:T(8,128)S(1)} fusion(f32[16,4096]{1,0:T(8,128)S(1)} %get-tuple-element.261, bf16[896,4096]{1,0:T(8,128)(2,1)} %get-tuple-element.274, bf16[16,4096]{1,0:T(8,128)(2,1)S(1)} %copy.20, s32[896]{0:T(1024)S(1)} %broadcast_subtract_fusion.2, f32[896]{0:T(1024)S(1)} %get-tuple-element.275), kind=kOutput, calls=%fused_computation.6.clone.1 | convolution fusion | flops 235098112 | bytes 8002560 | tf_op jit(solution)/shard_map/while/body/eval_jaxpr/dot_general | solution.py:30
  331.7 9.5 %collective-permute-done = bf16[16,4096]{1,0:T(8,128)(2,1)S(1)} collective-permute-done((bf16[16,4096]{1,0:T(8,128)(2,1)S(1)}, bf16[16,4096]{1,0:T(8,128)(2,1)S(1)}, u32[]{:S(2)}, u32[]{:S(2)}) %collective-permute-start) | collective-permute-done | bytes 131104 | tf_op jit(solution)/shard_map/while/body/eval_jaxpr/ppermute | solution.py:13
  341.2 6.6 %gather_fusion.1 = bf16[896,4096]{1,0:T(8,128)(2,1)} fusion(bf16[64,4096]{1,0:T(8,128)(2,1)S(1)} %all_gather.3, s32[1024]{0:T(1024)S(1)} %pad_clamp_fusion.1), kind=kCustom, calls=%fused_computation.1 | custom fusion | bytes 14683648 | tf_op jit(solution)/shard_map/gather | solution.py:110
  348.4 7.2 %multiply_convert_fusion = bf16[896,4096]{1,0:T(8,128)(2,1)} fusion(bf16[896,4096]{1,0:T(8,128)(2,1)} %gather_fusion.1, f32[896]{0:T(1024)S(1)} %get-tuple-element.296, pred[896]{0:T(1024)(128)(4,1)S(1)} %compare_and_fusion, bf16[64,4096]{1,0:T(8,128)(2,1)S(1)} %all_gather.3, f32[896,64]{0,1:T(8,128)S(1)} %get-tuple-element.203), kind=kOutput, calls=%fused_computation.23 | convolution fusion | flops 491839488 | bytes 15438208 | tf_op jit(solution)/shard_map/dot_general | solution.py:112
  (63 shorter events, 34.9 us)
Async XLA Ops:
  6.4 17.4 %all-to-all-start = ((s32[8,1,1]{2,1,0:T(1,128)}), s32[8,1,1]{2,1,0:T(1,128)S(1)}, u32[]{:S(2)}, u32[]{:S(2)}) async-start(s32[8,1,1]{2,1,0:T(1,128)} %copy.13), calls=%async_computation | async-start | bytes 8192 | tf_op jit(solution)/shard_map/all_to_all | solution.py:66
  21.9 49.9 %copy-start.2 = (f32[1024]{0:T(1024)S(1)}, f32[1024]{0:T(1024)}, u32[]{:S(2)}) copy-start(f32[1024]{0:T(1024)} %param.15) | copy-start | bytes 12292
  23.8 36.5 %all-to-all-start.1 = ((bf16[8,154,1024]{2,1,0:T(8,128)(2,1)}), bf16[8,154,1024]{2,1,0:T(8,128)(2,1)S(1)}, u32[]{:S(2)}, u32[]{:S(2)}) async-start(bf16[8,154,1024]{2,1,0:T(8,128)(2,1)} %reshape.207), calls=%async_computation.1 | async-start | bytes 5242880 | tf_op jit(solution)/shard_map/all_to_all | solution.py:65
  109.5 10.9 %copy-start.1 = (s32[896]{0:T(1024)S(1)}, s32[896]{0:T(1024)}, u32[]{:S(2)}) copy-start(s32[896]{0:T(1024)} %param.17) | copy-start | bytes 10756
  109.5 121.8 %all-to-all-start.2 = ((bf16[8,154,4096]{2,1,0:T(8,128)(2,1)}), bf16[8,154,4096]{2,1,0:T(8,128)(2,1)}, u32[]{:S(2)}, u32[]{:S(2)}) async-start(bf16[8,154,4096]{2,1,0:T(8,128)(2,1)} %broadcast_select_fusion), calls=%async_computation.2 | async-start | bytes 20971520 | tf_op jit(solution)/shard_map/all_to_all | solution.py:94
  243.4 22.1 %copy-start = (bf16[896,4096]{1,0:T(8,128)(2,1)S(1)}, bf16[896,4096]{1,0:T(8,128)(2,1)}, u32[]{:S(2)}) copy-start(bf16[896,4096]{1,0:T(8,128)(2,1)} %fusion.11) | copy-start | bytes 22020100
  276.7 9.6 %collective-permute-start.1 = (f32[16,4096]{1,0:T(8,128)S(1)}, f32[16,4096]{1,0:T(8,128)S(1)}, u32[]{:S(2)}, u32[]{:S(2)}) collective-permute-start(f32[16,4096]{1,0:T(8,128)S(1)} %fusion.59), channel_id=1, source_target_pairs={{0,1},{1,2},{2,3},{3,0},{4,5},{5,6},{6,7},{7,4},{8,9},{9,10},{10,1... | collective-permute-start | bytes 786440 | tf_op jit(solution)/shard_map/while/body/eval_jaxpr/ppermute | solution.py:13
  277.0 9.2 %collective-permute-start = (bf16[16,4096]{1,0:T(8,128)(2,1)S(1)}, bf16[16,4096]{1,0:T(8,128)(2,1)S(1)}, u32[]{:S(2)}, u32[]{:S(2)}) collective-permute-start(bf16[16,4096]{1,0:T(8,128)(2,1)S(1)} %copy.20), channel_id=1, source_target_pairs={{0,1},{1,2},{2,3},{3,0},{4,5},{5,6},{6,7},{7,4},{8,9},{9,10},{10,1... | collective-permute-start | bytes 393224 | tf_op jit(solution)/shard_map/while/body/eval_jaxpr/ppermute | solution.py:13
  295.0 9.6 %collective-permute-start.1 = (f32[16,4096]{1,0:T(8,128)S(1)}, f32[16,4096]{1,0:T(8,128)S(1)}, u32[]{:S(2)}, u32[]{:S(2)}) collective-permute-start(f32[16,4096]{1,0:T(8,128)S(1)} %fusion.59), channel_id=1, source_target_pairs={{0,1},{1,2},{2,3},{3,0},{4,5},{5,6},{6,7},{7,4},{8,9},{9,10},{10,1... | collective-permute-start | bytes 786440 | tf_op jit(solution)/shard_map/while/body/eval_jaxpr/ppermute | solution.py:13
  295.0 9.6 %collective-permute-start = (bf16[16,4096]{1,0:T(8,128)(2,1)S(1)}, bf16[16,4096]{1,0:T(8,128)(2,1)S(1)}, u32[]{:S(2)}, u32[]{:S(2)}) collective-permute-start(bf16[16,4096]{1,0:T(8,128)(2,1)S(1)} %copy.20), channel_id=1, source_target_pairs={{0,1},{1,2},{2,3},{3,0},{4,5},{5,6},{6,7},{7,4},{8,9},{9,10},{10,1... | collective-permute-start | bytes 393224 | tf_op jit(solution)/shard_map/while/body/eval_jaxpr/ppermute | solution.py:13
  313.3 9.6 %collective-permute-start.1 = (f32[16,4096]{1,0:T(8,128)S(1)}, f32[16,4096]{1,0:T(8,128)S(1)}, u32[]{:S(2)}, u32[]{:S(2)}) collective-permute-start(f32[16,4096]{1,0:T(8,128)S(1)} %fusion.59), channel_id=1, source_target_pairs={{0,1},{1,2},{2,3},{3,0},{4,5},{5,6},{6,7},{7,4},{8,9},{9,10},{10,1... | collective-permute-start | bytes 786440 | tf_op jit(solution)/shard_map/while/body/eval_jaxpr/ppermute | solution.py:13
  313.3 9.6 %collective-permute-start = (bf16[16,4096]{1,0:T(8,128)(2,1)S(1)}, bf16[16,4096]{1,0:T(8,128)(2,1)S(1)}, u32[]{:S(2)}, u32[]{:S(2)}) collective-permute-start(bf16[16,4096]{1,0:T(8,128)(2,1)S(1)} %copy.20), channel_id=1, source_target_pairs={{0,1},{1,2},{2,3},{3,0},{4,5},{5,6},{6,7},{7,4},{8,9},{9,10},{10,1... | collective-permute-start | bytes 393224 | tf_op jit(solution)/shard_map/while/body/eval_jaxpr/ppermute | solution.py:13
  331.7 9.6 %collective-permute-start.1 = (f32[16,4096]{1,0:T(8,128)S(1)}, f32[16,4096]{1,0:T(8,128)S(1)}, u32[]{:S(2)}, u32[]{:S(2)}) collective-permute-start(f32[16,4096]{1,0:T(8,128)S(1)} %fusion.59), channel_id=1, source_target_pairs={{0,1},{1,2},{2,3},{3,0},{4,5},{5,6},{6,7},{7,4},{8,9},{9,10},{10,1... | collective-permute-start | bytes 786440 | tf_op jit(solution)/shard_map/while/body/eval_jaxpr/ppermute | solution.py:13
  331.7 9.6 %collective-permute-start = (bf16[16,4096]{1,0:T(8,128)(2,1)S(1)}, bf16[16,4096]{1,0:T(8,128)(2,1)S(1)}, u32[]{:S(2)}, u32[]{:S(2)}) collective-permute-start(bf16[16,4096]{1,0:T(8,128)(2,1)S(1)} %copy.20), channel_id=1, source_target_pairs={{0,1},{1,2},{2,3},{3,0},{4,5},{5,6},{6,7},{7,4},{8,9},{9,10},{10,1... | collective-permute-start | bytes 393224 | tf_op jit(solution)/shard_map/while/body/eval_jaxpr/ppermute | solution.py:13
where the time goes:
time: 357 us; the launch traced here: 356 us
  waiting for transfers between devices  166 us (46%)
  local copies, waits for them, and re-layouts  69.4 us (19%)
  matrix products  57.2 us (16%)
  other arithmetic  29.9 us (8%)
  blocking collectives  16.4 us (5%)
  starting transfers between devices  16.1 us (5%)
    all_to_all x1, waiting for transfers between devices, on_device(): lax.all_to_all(outgoing, 'dp', split_axis=0, concat_axis=0, tiled=True)  97.3 us
    ppermute x8, waiting for transfers between devices, passed_along(): lax.ppermute(shard, axis, [(i, (i + by) % length) for i in range(length)])  36.8 us
    dot_general x4, matrix products, contract_first(): lax.dot_general(left_side, right_side, (((0,), (0,)), ((), ())), preferre...  34.8 us
    all_to_all x1, waiting for transfers between devices, on_device(): lax.all_to_all(send_rows, 'dp', split_axis=0, concat_axis=0, tiled=True)  31.5 us
    gather x2, local copies, waits for them, and re-layouts, on_device(): embedded[gather_at]  20.4 us
    all_gather x1, blocking collectives, on_device(): doc_piece = lax.all_gather(doc_unit, 'blk', axis=0, tiled=True)  16.4 us
    reshape x1, local copies, waits for them, and re-layouts, on_device(): returned.reshape(groups * capacity, emb_width)  12.2 us
    select_n x1, other arithmetic, on_device(): jnp.where(valid_slots.reshape(groups * capacity)[:, None], embedded[gathe...  9.97 us
  transfers between devices with their start and end apart: 11, of which 6 were waited for; matrix products, arithmetic and copies ran while one was open for 9% of the time, Pallas kernels for 0%

commit v1 on v0

--- a/solution.py
+++ b/solution.py
@@ -1,3 +1,4 @@
+import functools
 import jax
 import jax.numpy as jnp
 from jax import lax
@@ -6,6 +7,25 @@
 SESS_DEV = 16
 logit_scale = 20.0
 epsilon = 1e-06
+
+
+def report_field(piece_in, axis_k):
+    n_shards = jax.lax.axis_size("blk")
+    bank = tuple(((m, (m + 1) % n_shards) for m in range(n_shards)))
+
+    def treat_the_widths(block_next):
+        if len(block_next) == n_shards:
+            return block_next
+        u1 = jax.lax.ppermute(block_next[0], "blk", bank)
+        return treat_the_widths([u1, *block_next])
+
+    piece_next = treat_the_widths([piece_in])
+    k_now = jnp.concatenate(piece_next, axis=axis_k)
+    right_arr = jax.lax.axis_index("blk")
+    return jnp.roll(k_now, (right_arr + 1) * piece_in.shape[axis_k], axis=axis_k)
+
+
+wait_indices = functools.partial(report_field, axis_k=0)
 
 
 def passed_along(shard, axis, by):
@@ -101,7 +121,7 @@
     doc_unit = unit_rows(pooled)
     query_unit = unit_rows(queries)
     doc_rows = doc_unit.shape[0]
-    doc_piece = lax.all_gather(doc_unit, "blk", axis=0, tiled=True)
+    doc_piece = wait_indices(doc_unit)
     piece_rows = doc_piece.shape[0]
     logits = logit_scale * contract_rows(query_unit, doc_piece)
     weights = jnp.exp(logits)

time: 357 us -> 380 us (1.064)
  waiting for transfers between devices: 166 us -> 187 us
  blocking collectives: 16.4 us -> 0 us
  other arithmetic: 29.9 us -> 41.4 us
    all_gather x1 -> x0, blocking collectives: 16.4 us -> none  [on_device(): doc_piece = lax.all_gather(doc_unit, 'blk', axis=0, tiled=True)]
    convert_element_type x0 -> x1, other arithmetic: none -> 11.4 us  [on_device(): (logit_scale * (numerator / totals[:, None] - chosen_doc)).astype(jnp.bfl...]
    ppermute x0 -> x3, waiting for transfers between devices: none -> 11.1 us  [treat_the_widths(): u1 = jax.lax.ppermute(block_next[0], 'blk', bank)]
    all_to_all x1, waiting for transfers between devices: 97.3 us -> 106 us  [on_device(): lax.all_to_all(outgoing, 'dp', split_axis=0, concat_axis=0, tiled=True)]
    ppermute x0 -> x3, starting transfers between devices: none -> 4.19 us  [treat_the_widths(): u1 = jax.lax.ppermute(block_next[0], 'blk', bank)]
  transfers between devices with their start and end apart: 11 -> 14, of which waited for: 6 -> 8; matrix products, arithmetic and copies ran while one was open for 9% -> 8% of each run, Pallas kernels for 0% -> 0%
where the time goes in v1:
time: 380 us; the launch traced here: 379 us
  waiting for transfers between devices  187 us (49%)
  local copies, waits for them, and re-layouts  69.5 us (18%)
  matrix products  60.3 us (16%)
  other arithmetic  41.4 us (11%)
  starting transfers between devices  19.2 us (5%)
    all_to_all x1, waiting for transfers between devices, on_device(): lax.all_to_all(outgoing, 'dp', split_axis=0, concat_axis=0, tiled=True)  106 us
    ppermute x8, waiting for transfers between devices, passed_along(): lax.ppermute(shard, axis, [(i, (i + by) % length) for i in range(length)])  37.8 us
    dot_general x4, matrix products, contract_first(): lax.dot_general(left_side, right_side, (((0,), (0,)), ((), ())), preferre...  34.8 us
    all_to_all x1, waiting for transfers between devices, on_device(): lax.all_to_all(send_rows, 'dp', split_axis=0, concat_axis=0, tiled=True)  31.5 us
    gather x2, local copies, waits for them, and re-layouts, on_device(): embedded[gather_at]  20.4 us
    reshape x1, local copies, waits for them, and re-layouts, on_device(): returned.reshape(groups * capacity, emb_width)  12.2 us
    convert_element_type x1, other arithmetic, on_device(): (logit_scale * (numerator / totals[:, None] - chosen_doc)).astype(jnp.bfl...  11.4 us
    ppermute x3, waiting for transfers between devices, treat_the_widths(): u1 = jax.lax.ppermute(block_next[0], 'blk', bank)  11.1 us
  transfers between devices with their start and end apart: 14, of which 8 were waited for; matrix products, arithmetic and copies ran while one was open for 8% of the time, Pallas kernels for 0%

profile of v1, /device:TPU:0, one launch (start us, length us, event | category | flops | bytes accessed | tf_op | source)
XLA Modules:
  0.0 378.8 jit_solution(3239324119281498882)
XLA Ops:
  12.2 9.7 %scatter_custom_fusion.1 = bf16[1232,1024]{1,0:T(8,128)(2,1)S(1)} fusion(s32[1280]{0:T(1024)S(1)} %compare_select_fusion.2, bf16[1280,1024]{1,0:T(8,128)(2,1)} %param.10, bf16[]{:T(256)} %constant.128.clone.1), kind=kCustom, calls=%fused_computation.41 | custom fusion | bytes 2523648 | tf_op jit(solution)/shard_map/scatter | solution.py:78
  28.7 31.5 %all-to-all-done.1 = bf16[8,154,1024]{2,1,0:T(8,128)(2,1)S(1)} async-done(((bf16[8,154,1024]{2,1,0:T(8,128)(2,1)}), bf16[8,154,1024]{2,1,0:T(8,128)(2,1)S(1)}, u32[]{:S(2)}, u32[]{:S(2)}) %all-to-all-start.1) | async-done | bytes 2523168 | tf_op jit(solution)/shard_map/all_to_all | solution.py:85
  62.0 9.5 %scatter_custom_fusion.2 = bf16[320,1024]{1,0:T(8,128)(2,1)S(1)} fusion(s32[1232]{0:T(1024)S(1)} %get-tuple-element.186, bf16[1232,1024]{1,0:T(8,128)(2,1)} %reshape.246, bf16[]{:T(256)} %constant.128.clone.1), kind=kCustom, calls=%fused_computation.46 | custom fusion | bytes 655872 | tf_op jit(solution)/shard_map/scatter | solution.py:96
  71.8 7.3 %fusion.21 = bf16[320,4096]{1,0:T(8,128)(2,1)S(1)} fusion(bf16[1,1024,4096]{2,1,0:T(8,128)(2,1)} %param.14, bf16[320,1024]{1,0:T(8,128)(2,1)S(1)} %scatter_custom_fusion.2, f32[1024]{0:T(1024)S(1)} %copy-done.1, f32[320]{0:T(512)S(1)} %add_rsqrt_fusion.1), kind=kOutput, calls=%fused_computation.35 | convolution fusion | flops 2697461760 | bytes 11670784 | tf_op jit(solution)/shard_map/dot_general | solution.py:105
  79.1 8.2 %gather_fusion = bf16[1232,4096]{1,0:T(8,128)(2,1)} fusion(bf16[320,4096]{1,0:T(8,128)(2,1)S(1)} %fusion.21, s32[2048]{0:T(1024)S(1)} %pad_clamp_fusion), kind=kCustom, calls=%fused_computation | custom fusion | bytes 20190016 | tf_op jit(solution)/shard_map/gather | solution.py:111
  87.4 12.1 %gather.9 = bf16[8,154,4096]{2,1,0:T(8,128)(2,1)} reshape(bf16[1232,4096]{1,0:T(8,128)(2,1)} %gather_fusion) | data formatting | bytes 20185088 | tf_op jit(solution)/shard_map/gather | solution.py:111
  99.5 10.0 %broadcast_select_fusion = bf16[8,154,4096]{2,1,0:T(8,128)(2,1)} fusion(bf16[8,154,4096]{2,1,0:T(8,128)(2,1)} %gather.9, pred[8,154]{1,0:T(8,128)(4,1)S(1)} %iota_compare_fusion.7), kind=kLoop, calls=%fused_computation.24 | loop fusion | flops 5046272 | bytes 20186320 | tf_op jit(solution)/shard_map/jit(_where)/select_n | solution.py:109
  114.6 5.6 %scatter_custom_fusion = s32[1232]{0:T(1024)S(1)} fusion(s32[1280]{0:T(1024)S(1)} %compare_select_fusion.2, s32[1280]{0:T(1024)} %param.12, s32[]{:T(128)} %constant.123.clone.1), kind=kCustom, calls=%fused_computation.91 | custom fusion | bytes 5440 | tf_op jit(solution)/shard_map/scatter | solution.py:82
  124.8 106.3 %all-to-all-done.2 = bf16[8,154,4096]{2,1,0:T(8,128)(2,1)} async-done(((bf16[8,154,4096]{2,1,0:T(8,128)(2,1)}), bf16[8,154,4096]{2,1,0:T(8,128)(2,1)}, u32[]{:S(2)}, u32[]{:S(2)}) %all-to-all-start.2) | async-done | bytes 10092576 | tf_op jit(solution)/shard_map/all_to_all | solution.py:114
  231.2 12.2 %reshape.209 = bf16[1232,4096]{1,0:T(8,128)(2,1)} reshape(bf16[8,154,4096]{2,1,0:T(8,128)(2,1)} %all-to-all-done.2) | data formatting | bytes 20185088 | tf_op jit(solution)/shard_map/reshape | solution.py:119
  250.4 8.9 %fusion.11 = bf16[896,4096]{1,0:T(8,128)(2,1)} fusion(bf16[896,4096]{1,0:T(8,128)(2,1)} %param.16, f32[896]{0:T(1024)S(1)} %add_rsqrt_fusion), kind=kLoop, calls=%fused_computation.22 | loop fusion | flops 11010048 | bytes 14683648 | tf_op jit(solution)/shard_map/convert_element_type | solution.py:40
  267.3 5.8 %collective-permute-done.4 = bf16[16,4096]{1,0:T(8,128)(2,1)S(1)} collective-permute-done((bf16[16,4096]{1,0:T(8,128)(2,1)S(1)}, bf16[16,4096]{1,0:T(8,128)(2,1)S(1)}, u32[]{:S(2)}, u32[]{:S(2)}) %collective-permute-start.4) | collective-permute-done | bytes 131104 | tf_op jit(solution)/shard_map/ppermute | solution.py:19
  278.9 73.3 %while.17 = (s32[]{:T(128)}, bf16[16,4096]{1,0:T(8,128)(2,1)S(1)}, f32[16,4096]{1,0:T(8,128)S(1)}, bf16[896,4096]{1,0:T(8,128)(2,1)}, f32[896]{0:T(1024)S(1)}, /...) while((s32[]{:T(128)}, bf16[16,4096]{1,0:T(8,128)(2,1)S(1)}, ...), condition=%wide.region_14.15_spmd, body=%wide.region_13.14_spmd.sunk | while | flops 235099024 | bytes 9845070 | solution.py:151
  278.9 8.7 %fusion.60 = f32[16,4096]{1,0:T(8,128)S(1)} fusion(f32[16,4096]{1,0:T(8,128)S(1)} %get-tuple-element.261, bf16[896,4096]{1,0:T(8,128)(2,1)} %get-tuple-element.274, bf16[16,4096]{1,0:T(8,128)(2,1)S(1)} %copy.27, s32[896]{0:T(1024)S(1)} %broadcast_subtract_fusion.2, f32[896]{0:T(1024)S(1)} %get-tuple-element.275), kind=kOutput, calls=%fused_computation.6.clone.1 | convolution fusion | flops 235098112 | bytes 8002560 | tf_op jit(solution)/shard_map/while/body/eval_jaxpr/dot_general | solution.py:50
  287.9 9.3 %collective-permute-done = bf16[16,4096]{1,0:T(8,128)(2,1)S(1)} collective-permute-done((bf16[16,4096]{1,0:T(8,128)(2,1)S(1)}, bf16[16,4096]{1,0:T(8,128)(2,1)S(1)}, u32[]{:S(2)}, u32[]{:S(2)}) %collective-permute-start) | collective-permute-done | bytes 131104 | tf_op jit(solution)/shard_map/while/body/eval_jaxpr/ppermute | solution.py:33
  297.3 8.7 %fusion.60 = f32[16,4096]{1,0:T(8,128)S(1)} fusion(f32[16,4096]{1,0:T(8,128)S(1)} %get-tuple-element.261, bf16[896,4096]{1,0:T(8,128)(2,1)} %get-tuple-element.274, bf16[16,4096]{1,0:T(8,128)(2,1)S(1)} %copy.27, s32[896]{0:T(1024)S(1)} %broadcast_subtract_fusion.2, f32[896]{0:T(1024)S(1)} %get-tuple-element.275), kind=kOutput, calls=%fused_computation.6.clone.1 | convolution fusion | flops 235098112 | bytes 8002560 | tf_op jit(solution)/shard_map/while/body/eval_jaxpr/dot_general | solution.py:50
  306.0 9.5 %collective-permute-done = bf16[16,4096]{1,0:T(8,128)(2,1)S(1)} collective-permute-done((bf16[16,4096]{1,0:T(8,128)(2,1)S(1)}, bf16[16,4096]{1,0:T(8,128)(2,1)S(1)}, u32[]{:S(2)}, u32[]{:S(2)}) %collective-permute-start) | collective-permute-done | bytes 131104 | tf_op jit(solution)/shard_map/while/body/eval_jaxpr/ppermute | solution.py:33
  315.6 8.7 %fusion.60 = f32[16,4096]{1,0:T(8,128)S(1)} fusion(f32[16,4096]{1,0:T(8,128)S(1)} %get-tuple-element.261, bf16[896,4096]{1,0:T(8,128)(2,1)} %get-tuple-element.274, bf16[16,4096]{1,0:T(8,128)(2,1)S(1)} %copy.27, s32[896]{0:T(1024)S(1)} %broadcast_subtract_fusion.2, f32[896]{0:T(1024)S(1)} %get-tuple-element.275), kind=kOutput, calls=%fused_computation.6.clone.1 | convolution fusion | flops 235098112 | bytes 8002560 | tf_op jit(solution)/shard_map/while/body/eval_jaxpr/dot_general | solution.py:50
  324.3 9.5 %collective-permute-done = bf16[16,4096]{1,0:T(8,128)(2,1)S(1)} collective-permute-done((bf16[16,4096]{1,0:T(8,128)(2,1)S(1)}, bf16[16,4096]{1,0:T(8,128)(2,1)S(1)}, u32[]{:S(2)}, u32[]{:S(2)}) %collective-permute-start) | collective-permute-done | bytes 131104 | tf_op jit(solution)/shard_map/while/body/eval_jaxpr/ppermute | solution.py:33
  333.9 8.7 %fusion.60 = f32[16,4096]{1,0:T(8,128)S(1)} fusion(f32[16,4096]{1,0:T(8,128)S(1)} %get-tuple-element.261, bf16[896,4096]{1,0:T(8,128)(2,1)} %get-tuple-element.274, bf16[16,4096]{1,0:T(8,128)(2,1)S(1)} %copy.27, s32[896]{0:T(1024)S(1)} %broadcast_subtract_fusion.2, f32[896]{0:T(1024)S(1)} %get-tuple-element.275), kind=kOutput, calls=%fused_computation.6.clone.1 | convolution fusion | flops 235098112 | bytes 8002560 | tf_op jit(solution)/shard_map/while/body/eval_jaxpr/dot_general | solution.py:50
  342.7 9.5 %collective-permute-done = bf16[16,4096]{1,0:T(8,128)(2,1)S(1)} collective-permute-done((bf16[16,4096]{1,0:T(8,128)(2,1)S(1)}, bf16[16,4096]{1,0:T(8,128)(2,1)S(1)}, u32[]{:S(2)}, u32[]{:S(2)}) %collective-permute-start) | collective-permute-done | bytes 131104 | tf_op jit(solution)/shard_map/while/body/eval_jaxpr/ppermute | solution.py:33
  352.2 7.3 %fusion.34 = f32[896,4096]{1,0:T(8,128)} fusion(bf16[64,4096]{1,0:T(8,128)(2,1)S(1)} %constant_dynamic-slice_fusion, f32[896,64]{0,1:T(8,128)S(1)} %get-tuple-element.203), kind=kOutput, calls=%fused_computation.54 | convolution fusion | flops 469819392 | bytes 15433728 | tf_op jit(solution)/shard_map/dot_general | solution.py:132
  359.5 6.6 %gather_fusion.1 = bf16[896,4096]{1,0:T(8,128)(2,1)} fusion(bf16[64,4096]{1,0:T(8,128)(2,1)S(1)} %constant_dynamic-slice_fusion, s32[1024]{0:T(1024)S(1)} %pad_clamp_fusion.1), kind=kCustom, calls=%fused_computation.1 | custom fusion | bytes 14683648 | tf_op jit(solution)/shard_map/gather | solution.py:130
  366.7 11.4 %multiply_convert_fusion = bf16[896,4096]{1,0:T(8,128)(2,1)} fusion(bf16[896,4096]{1,0:T(8,128)(2,1)} %gather_fusion.1, f32[896,4096]{1,0:T(8,128)} %fusion.34, f32[896]{0:T(1024)S(1)} %get-tuple-element.302, pred[896]{0:T(1024)(128)(4,1)S(1)} %compare_and_fusion), kind=kLoop, calls=%fused_computation.23 | loop fusion | flops 22020096 | bytes 29364608 | tf_op jit(solution)/shard_map/convert_element_type | solution.py:155
  (76 shorter events, 52.1 us)
Async XLA Ops:
  6.4 17.4 %all-to-all-start = ((s32[8,1,1]{2,1,0:T(1,128)}), s32[8,1,1]{2,1,0:T(1,128)S(1)}, u32[]{:S(2)}, u32[]{:S(2)}) async-start(s32[8,1,1]{2,1,0:T(1,128)} %copy.13), calls=%async_computation | async-start | bytes 8192 | tf_op jit(solution)/shard_map/all_to_all | solution.py:86
  21.9 49.9 %copy-start.1 = (f32[1024]{0:T(1024)S(1)}, f32[1024]{0:T(1024)}, u32[]{:S(2)}) copy-start(f32[1024]{0:T(1024)} %param.15) | copy-start | bytes 12292
  23.8 36.5 %all-to-all-start.1 = ((bf16[8,154,1024]{2,1,0:T(8,128)(2,1)}), bf16[8,154,1024]{2,1,0:T(8,128)(2,1)S(1)}, u32[]{:S(2)}, u32[]{:S(2)}) async-start(bf16[8,154,1024]{2,1,0:T(8,128)(2,1)} %reshape.207), calls=%async_computation.1 | async-start | bytes 5242880 | tf_op jit(solution)/shard_map/all_to_all | solution.py:85
  109.5 121.7 %all-to-all-start.2 = ((bf16[8,154,4096]{2,1,0:T(8,128)(2,1)}), bf16[8,154,4096]{2,1,0:T(8,128)(2,1)}, u32[]{:S(2)}, u32[]{:S(2)}) async-start(bf16[8,154,4096]{2,1,0:T(8,128)(2,1)} %broadcast_select_fusion), calls=%async_computation.2 | async-start | bytes 20971520 | tf_op jit(solution)/shard_map/all_to_all | solution.py:114
  248.8 12.2 %copy-start = (s32[896]{0:T(1024)S(1)}, s32[896]{0:T(1024)}, u32[]{:S(2)}) copy-start(s32[896]{0:T(1024)} %param.17) | copy-start | bytes 10756
  248.8 10.6 %collective-permute-start.2 = (bf16[16,4096]{1,0:T(8,128)(2,1)S(1)}, bf16[16,4096]{1,0:T(8,128)(2,1)S(1)}, u32[]{:S(2)}, u32[]{:S(2)}) collective-permute-start(bf16[16,4096]{1,0:T(8,128)(2,1)S(1)} %multiply_convert_fusion.1), channel_id=1, source_target_pairs={{0,1},{1,2},{2,3},{3,0},{4,5},{5,6},{6,7},{7,4},{8,9},{9,10},{10,1... | collective-permute-start | bytes 393224 | tf_op jit(solution)/shard_map/ppermute | solution.py:19
  259.4 6.9 %collective-permute-start.3 = (bf16[16,4096]{1,0:T(8,128)(2,1)S(1)}, bf16[16,4096]{1,0:T(8,128)(2,1)S(1)}, u32[]{:S(2)}, u32[]{:S(2)}) collective-permute-start(bf16[16,4096]{1,0:T(8,128)(2,1)S(1)} %collective-permute-done.2), channel_id=1, source_target_pairs={{0,1},{1,2},{2,3},{3,0},{4,5},{5,6},{6,7},{7,4},{8,9},{9,10},{10,1... | collective-permute-start | bytes 393224 | tf_op jit(solution)/shard_map/ppermute | solution.py:19
  266.3 6.8 %collective-permute-start.4 = (bf16[16,4096]{1,0:T(8,128)(2,1)S(1)}, bf16[16,4096]{1,0:T(8,128)(2,1)S(1)}, u32[]{:S(2)}, u32[]{:S(2)}) collective-permute-start(bf16[16,4096]{1,0:T(8,128)(2,1)S(1)} %collective-permute-done.3), channel_id=1, source_target_pairs={{0,1},{1,2},{2,3},{3,0},{4,5},{5,6},{6,7},{7,4},{8,9},{9,10},{10,1... | collective-permute-start | bytes 393224 | tf_op jit(solution)/shard_map/ppermute | solution.py:19
  287.6 9.6 %collective-permute-start.1 = (f32[16,4096]{1,0:T(8,128)S(1)}, f32[16,4096]{1,0:T(8,128)S(1)}, u32[]{:S(2)}, u32[]{:S(2)}) collective-permute-start(f32[16,4096]{1,0:T(8,128)S(1)} %fusion.60), channel_id=1, source_target_pairs={{0,1},{1,2},{2,3},{3,0},{4,5},{5,6},{6,7},{7,4},{8,9},{9,10},{10,1... | collective-permute-start | bytes 786440 | tf_op jit(solution)/shard_map/while/body/eval_jaxpr/ppermute | solution.py:33
  287.6 9.6 %collective-permute-start = (bf16[16,4096]{1,0:T(8,128)(2,1)S(1)}, bf16[16,4096]{1,0:T(8,128)(2,1)S(1)}, u32[]{:S(2)}, u32[]{:S(2)}) collective-permute-start(bf16[16,4096]{1,0:T(8,128)(2,1)S(1)} %copy.27), channel_id=1, source_target_pairs={{0,1},{1,2},{2,3},{3,0},{4,5},{5,6},{6,7},{7,4},{8,9},{9,10},{10,1... | collective-permute-start | bytes 393224 | tf_op jit(solution)/shard_map/while/body/eval_jaxpr/ppermute | solution.py:33
  306.0 9.6 %collective-permute-start.1 = (f32[16,4096]{1,0:T(8,128)S(1)}, f32[16,4096]{1,0:T(8,128)S(1)}, u32[]{:S(2)}, u32[]{:S(2)}) collective-permute-start(f32[16,4096]{1,0:T(8,128)S(1)} %fusion.60), channel_id=1, source_target_pairs={{0,1},{1,2},{2,3},{3,0},{4,5},{5,6},{6,7},{7,4},{8,9},{9,10},{10,1... | collective-permute-start | bytes 786440 | tf_op jit(solution)/shard_map/while/body/eval_jaxpr/ppermute | solution.py:33
  306.0 9.6 %collective-permute-start = (bf16[16,4096]{1,0:T(8,128)(2,1)S(1)}, bf16[16,4096]{1,0:T(8,128)(2,1)S(1)}, u32[]{:S(2)}, u32[]{:S(2)}) collective-permute-start(bf16[16,4096]{1,0:T(8,128)(2,1)S(1)} %copy.27), channel_id=1, source_target_pairs={{0,1},{1,2},{2,3},{3,0},{4,5},{5,6},{6,7},{7,4},{8,9},{9,10},{10,1... | collective-permute-start | bytes 393224 | tf_op jit(solution)/shard_map/while/body/eval_jaxpr/ppermute | solution.py:33
  324.3 9.6 %collective-permute-start.1 = (f32[16,4096]{1,0:T(8,128)S(1)}, f32[16,4096]{1,0:T(8,128)S(1)}, u32[]{:S(2)}, u32[]{:S(2)}) collective-permute-start(f32[16,4096]{1,0:T(8,128)S(1)} %fusion.60), channel_id=1, source_target_pairs={{0,1},{1,2},{2,3},{3,0},{4,5},{5,6},{6,7},{7,4},{8,9},{9,10},{10,1... | collective-permute-start | bytes 786440 | tf_op jit(solution)/shard_map/while/body/eval_jaxpr/ppermute | solution.py:33
  324.3 9.6 %collective-permute-start = (bf16[16,4096]{1,0:T(8,128)(2,1)S(1)}, bf16[16,4096]{1,0:T(8,128)(2,1)S(1)}, u32[]{:S(2)}, u32[]{:S(2)}) collective-permute-start(bf16[16,4096]{1,0:T(8,128)(2,1)S(1)} %copy.27), channel_id=1, source_target_pairs={{0,1},{1,2},{2,3},{3,0},{4,5},{5,6},{6,7},{7,4},{8,9},{9,10},{10,1... | collective-permute-start | bytes 393224 | tf_op jit(solution)/shard_map/while/body/eval_jaxpr/ppermute | solution.py:33
  342.6 9.6 %collective-permute-start.1 = (f32[16,4096]{1,0:T(8,128)S(1)}, f32[16,4096]{1,0:T(8,128)S(1)}, u32[]{:S(2)}, u32[]{:S(2)}) collective-permute-start(f32[16,4096]{1,0:T(8,128)S(1)} %fusion.60), channel_id=1, source_target_pairs={{0,1},{1,2},{2,3},{3,0},{4,5},{5,6},{6,7},{7,4},{8,9},{9,10},{10,1... | collective-permute-start | bytes 786440 | tf_op jit(solution)/shard_map/while/body/eval_jaxpr/ppermute | solution.py:33
  342.6 9.6 %collective-permute-start = (bf16[16,4096]{1,0:T(8,128)(2,1)S(1)}, bf16[16,4096]{1,0:T(8,128)(2,1)S(1)}, u32[]{:S(2)}, u32[]{:S(2)}) collective-permute-start(bf16[16,4096]{1,0:T(8,128)(2,1)S(1)} %copy.27), channel_id=1, source_target_pairs={{0,1},{1,2},{2,3},{3,0},{4,5},{5,6},{6,7},{7,4},{8,9},{9,10},{10,1... | collective-permute-start | bytes 393224 | tf_op jit(solution)/shard_map/while/body/eval_jaxpr/ppermute | solution.py:33
